TPU v7x, 512 devices: a whole 4x4x16 slice. The times are simulated.
512 devices in a mesh: rows: 128 (over z, y, core), cols: 4 (over x).
Axes of the slice: x: 4, y: 4, z: 16, core: 2. Of those that a mesh axis runs over, the one named last changes fastest.
Arguments:
- features: bfloat16 [256, 16384], P('cols', 'rows'), may hold values from -6 to 6
- weight_matrix: bfloat16 [256, 256], replicated, may hold values from -0.375 to 0.375
- bias_vector: float32 [256], replicated, may hold values from -3 to 3
- adjacency_tiles: bfloat16 [128, 65, 128, 128], P('rows')
- tile_cols: int32 [128, 65], P('rows'), may hold values from 0 to 127, as said below
- tile_count: int32 [128], P('rows'), may hold values from 25 to 65, as said below
- out_grad: bfloat16 [256, 16384], P('cols', 'rows'), may hold values from -6 to 6
Outputs:
- layer_out: bfloat16 [256, 16384], P('cols', 'rows')
- feature_grad: bfloat16 [256, 16384], P('cols', 'rows')
- weight_grad: float32 [256, 256], P('cols')
- bias_grad: float32 [256], P('cols')
Inputs may be any that keep to these rules, and one draw needn't show every extreme that they name: `tile_cols`: the live slots of a row block name distinct column blocks, its own among them; the pattern is symmetric: c is live in row block b exactly when b is live in row block c, and that tile is the transpose of the one of b in c's list. Slots past tile_count hold the row block's own index. Outside the hub's row, every live column block other than the hub lies within 16 blocks of the row block around the cycle of 128 blocks; the hub's own row also holds such band blocks. `tile_count`: exactly one row block, the hub, has all 65 slots live.
All inputs are finite; a program needn't handle non-finite values.
Results may differ from a plain program's by a relative error of at most 0.008.
Values may be sent and summed in bfloat16 or wider, within the bound.
No kernel may reach another device: no remote copies, remote signals or barrier semaphores. Data moves between devices by JAX's collectives and lax.ppermute only.
A program may use at most 64 MiB of HBM per device.

v0:
```python
import math
import jax
import jax.numpy as jnp
from jax import lax
from jax.sharding import PartitionSpec as P


def block_products(panel_rows, adjacency_tiles, tile_cols, alive_mask):
    feature_width = panel_rows.shape[0]
    tile_side = adjacency_tiles.shape[-1]
    panel_grid = panel_rows.reshape(feature_width, -1, tile_side)
    picked = jnp.take(panel_grid, tile_cols, axis=1)
    picked = jnp.where(alive_mask[None, :, :, None], picked, jnp.zeros((), jnp.bfloat16))
    result = jnp.einsum(
        "fbsk,bsrk->fbr", picked, adjacency_tiles, preferred_element_type=jnp.float32
    )
    return result.reshape(feature_width, -1)


def per_device(
    features, weight_matrix, bias_vector, adjacency_tiles, tile_cols, tile_count, out_grad
):
    feature_width, rows_here = features.shape
    blocks_here, slot_count = tile_cols.shape
    tile_side = adjacency_tiles.shape[-1]
    column_index = lax.axis_index("cols")
    rows_count = lax.axis_size("rows")
    alive_mask = jnp.arange(slot_count, dtype=jnp.int32)[None, :] < tile_count[:, None]
    all_panels = lax.all_gather(features, "rows", axis=1, tiled=True)
    aggregated = block_products(all_panels, adjacency_tiles, tile_cols, alive_mask).astype(
        jnp.bfloat16
    )
    aggregated_full = lax.all_gather(aggregated, "cols", axis=0, tiled=True)
    weight_rows = lax.dynamic_slice_in_dim(
        weight_matrix, column_index * feature_width, feature_width, 0
    )
    bias_rows = lax.dynamic_slice_in_dim(
        bias_vector, column_index * feature_width, feature_width, 0
    )
    preact = (
        jnp.dot(weight_rows, aggregated_full, preferred_element_type=jnp.float32)
        + bias_rows[:, None]
    )
    sigmoid_pre = jax.nn.sigmoid(preact)
    layer_out = (preact * sigmoid_pre).astype(jnp.bfloat16)
    pre_grad = (
        out_grad.astype(jnp.float32) * sigmoid_pre * (1.0 + preact * (1.0 - sigmoid_pre))
    ).astype(jnp.bfloat16)
    partial_grad = jnp.einsum(
        "oi,on->in", weight_rows, pre_grad, preferred_element_type=jnp.float32
    )
    agg_grad = lax.psum_scatter(partial_grad, "cols", scatter_dimension=0, tiled=True).astype(
        jnp.bfloat16
    )
    grad_scale = 1.0 / math.sqrt(rows_here * rows_count)
    weight_part = (
        jnp.einsum("fn,in->fi", pre_grad, aggregated_full, preferred_element_type=jnp.float32)
        * grad_scale
    )
    bias_part = jnp.sum(pre_grad.astype(jnp.float32), axis=1) * grad_scale
    weight_grad, bias_grad = lax.psum((weight_part, bias_part), "rows")
    own_blocks = agg_grad.reshape(feature_width, blocks_here, tile_side)
    contrib_terms = jnp.einsum(
        "fbr,bsrk->bsfk", own_blocks, adjacency_tiles, preferred_element_type=jnp.float32
    )
    contrib_terms = contrib_terms * alive_mask[:, :, None, None].astype(jnp.float32)
    flat_terms = contrib_terms.reshape(-1, feature_width, tile_side)
    row_count = blocks_here * lax.axis_size("rows")
    inside = (tile_cols >= 0) & (tile_cols < row_count)
    target = jnp.where(inside, tile_cols, row_count).reshape(-1)
    empty = jnp.zeros((row_count, feature_width, tile_side), jnp.float32)
    gathered_grad = lax.psum_scatter(
        empty.at[target].add(flat_terms, mode="drop"), "rows", scatter_dimension=0, tiled=True
    )
    feature_grad = (
        gathered_grad.transpose(1, 0, 2).reshape(feature_width, rows_here).astype(jnp.bfloat16)
    )
    return (layer_out, feature_grad, weight_grad, bias_grad)


def solution(mesh):
    return jax.shard_map(
        per_device,
        mesh=mesh,
        in_specs=(
            P("cols", "rows"),
            P(),
            P(),
            P("rows", None, None, None),
            P("rows", None),
            P("rows"),
            P("cols", "rows"),
        ),
        out_specs=(P("cols", "rows"), P("cols", "rows"), P("cols", None), P("cols")),
        check_vma=False,
    )
```

profile of v0, /device:TPU:1, one launch (start us, length us, event | category | flops | bytes accessed | tf_op | source)
XLA Modules:
  0.0 802.5 jit_solution(16811597391701644600)
XLA Ops:
  7.2 0.7 all-gather.2.cloned.1.call-update
  7.9 0.0 reduce-scatter.3.cloned.1.call-start
  8.6 0.8 dynamic_slice.7
  9.4 0.7 fusion.31
  10.0 0.7 and_bitcast_fusion
  10.7 139.1 %all-gather.2.cloned.1.call-done = bf16[64,16384]{1,0:T(8,128)(2,1)} async-done(((bf16[64,128]{1,0:T(8,128)(2,1)}), bf16[64,16384]{1,0:T(8,128)(2,1)}) %all-gather.2.cloned.1.call-update) | async-done | bytes 2097168 | tf_op jit(solution)/shard_map/all_gather | solution.py:29
  149.8 3.5 copy_bitcast_fusion
  153.3 2.3 gather_fusion
  155.7 0.9 fusion.10
  156.6 9.2 %all_gather.7 = bf16[256,128]{1,0:T(8,128)(2,1)S(1)} all-gather(bf16[64,128]{1,0:T(8,128)(2,1)S(1)} %fusion.10), channel_id=1, replica_groups=mesh['rows'=128,'cols'=4] {'cols'}, dimensions={0}, use_global_device_ids=true | all-gather | bytes 81920 | tf_op jit(solution)/shard_map/all_gather | solution.py:33
  165.8 0.9 convert_reduce_fusion
  166.7 0.8 fusion.20
  167.5 0.0 reduce-scatter.5.cloned.1.call-start
  167.6 23.7 %reduce-scatter.3.cloned.1.call-done = f32[64,128]{1,0:T(8,128)} async-done(((f32[256,128]{1,0:T(8,128)}), f32[64,128]{1,0:T(8,128)}) %reduce-scatter.3.cloned.1.call-update) | async-done | bytes 32784 | tf_op jit(solution)/shard_map/reduce_scatter | solution.py:52
  191.3 2.5 fusion
  193.8 2.5 broadcast_in_dim.40
  196.3 12.6 %scatter_fusion = f32[128,64,128]{2,1,0:T(8,128)} fusion(f32[128,64,128]{2,1,0:T(8,128)} %broadcast_in_dim.40, s32[65]{0:T(128)S(1)} %fusion.26, f32[65,64,128]{2,1,0:T(8,128)} %fusion), kind=kCustom, calls=%fused_computation.1 | custom fusion | flops 532480 | bytes 6390020 | tf_op jit(solution)/shard_map/scatter-add | solution.py:73
  209.0 0.0 all-reduce.2.cloned.1.call-start
  209.0 251.3 %psum.15 = f32[64]{0:T(128)} all-reduce(f32[64]{0:T(128)S(1)} %broadcast_multiply_fusion), channel_id=1, replica_groups=mesh['rows'=128,'cols'=4] {'rows'}, use_global_device_ids=true, to_apply=%region_5.6 | all-reduce | flops 64 | bytes 512 | tf_op jit(solution)/shard_map/psum | solution.py:61
  460.3 0.8 convolution_multiply_fusion
  461.1 6.1 reduce-scatter.5.cloned.1.call-done
  467.2 1.4 convert_bitcast_fusion
  468.6 325.9 %all-reduce.2.cloned.1.call-done = f32[64,256]{1,0:T(8,128)} async-done(((f32[64,256]{1,0:T(8,128)}), f32[64,256]{1,0:T(8,128)}) %all-reduce.2.cloned.1.call-update) | async-done | bytes 65552 | tf_op jit(solution)/shard_map/psum | solution.py:61
  794.5 1.5 copy.17
  (17 shorter events, 0.1 us)
Async XLA Ops:
  7.2 148.5 %copy-start = (bf16[1,65,128,128]{3,2,1,0:T(8,128)(2,1)S(1)}, bf16[1,65,128,128]{3,2,1,0:T(8,128)(2,1)}, u32[]{:S(2)}) copy-start(bf16[1,65,128,128]{3,2,1,0:T(8,128)(2,1)} %param.10) | copy-start | bytes 6389764
  7.2 142.6 %all-gather.2.cloned.1.call-start = ((), (), s32[]{:S(2)}) async-start(), calls=%async_computation.2 | async-start | bytes 2113536 | tf_op jit(solution)/shard_map/all_gather | solution.py:29
  7.9 183.4 %reduce-scatter.3.cloned.1.call-start = ((), (), s32[]{:S(2)}) async-start(), calls=%async_computation.3 | async-start | bytes 163840 | tf_op jit(solution)/shard_map/reduce_scatter | solution.py:52
  155.6 10.2 %copy-start.1 = (bf16[256,256]{1,0:T(8,128)(2,1)S(1)}, bf16[256,256]{1,0:T(8,128)(2,1)}, u32[]{:S(2)}) copy-start(bf16[256,256]{1,0:T(8,128)(2,1)} %param.8) | copy-start | bytes 393220
  155.6 10.2 %copy-start.2 = (bf16[64,128]{1,0:T(8,128)(2,1)S(1)}, bf16[64,128]{1,0:T(8,128)(2,1)}, u32[]{:S(2)}) copy-start(bf16[64,128]{1,0:T(8,128)(2,1)} %param.13) | copy-start | bytes 49156
  155.7 12.0 %copy-start.3 = (s32[1,65]{1,0:T(1,128)S(1)}, s32[1,65]{1,0:T(1,128)}, u32[]{:S(2)}) copy-start(s32[1,65]{1,0:T(1,128)} %param.11) | copy-start | bytes 784
  167.5 299.6 %reduce-scatter.5.cloned.1.call-start = ((), (), s32[]{:S(2)}) async-start(), calls=%async_computation.4 | async-start | bytes 4227072 | tf_op jit(solution)/shard_map/reduce_scatter | solution.py:72
  209.0 585.5 %all-reduce.2.cloned.1.call-start = ((), (), s32[]{:S(2)}) async-start(), calls=%async_computation.5 | async-start | bytes 131072 | tf_op jit(solution)/shard_map/psum | solution.py:61
Sparse Core Ops, SparseCore 0:
  11.0 138.7 all-gather.1
  167.7 23.6 reduce-scatter.2
  209.1 258.0 reduce-scatter.4
  471.1 323.3 all-reduce.1
where the time goes:
time: 803 us; the launch traced here: 802 us
  waiting for transfers between devices  496 us (62%)
  blocking collectives  261 us (33%)
  other arithmetic  15.3 us (2%)
  between operations  14.5 us (2%)
  local copies, waits for them, and re-layouts  10.5 us (1%)
    psum x1, waiting for transfers between devices, per_device(): weight_grad, bias_grad = lax.psum((weight_part, bias_part), 'rows')  326 us
    psum x1, blocking collectives, per_device(): weight_grad, bias_grad = lax.psum((weight_part, bias_part), 'rows')  251 us
    all_gather x1, waiting for transfers between devices, per_device(): all_panels = lax.all_gather(features, 'rows', axis=1, tiled=True)  139 us
    reduce_scatter x1, waiting for transfers between devices, per_device(): lax.psum_scatter(partial_grad, 'cols', scatter_dimension=0, tiled=True)  23.7 us
  transfers between devices with their start and end apart: 4, of which 4 were waited for; matrix products, arithmetic and copies ran while one was open for 1% of the time, Pallas kernels for 0%

commit v1 on v0

--- a/solution.py
+++ b/solution.py
@@ -26,7 +26,9 @@
     column_index = lax.axis_index("cols")
     rows_count = lax.axis_size("rows")
     alive_mask = jnp.arange(slot_count, dtype=jnp.int32)[None, :] < tile_count[:, None]
-    all_panels = lax.all_gather(features, "rows", axis=1, tiled=True)
+    all_panels = jnp.concatenate(
+        lax.all_to_all(jnp.stack([features] * lax.axis_size("rows")), "rows", 0, 0), axis=1
+    )
     aggregated = block_products(all_panels, adjacency_tiles, tile_cols, alive_mask).astype(
         jnp.bfloat16
     )

time: 803 us -> 778 us (0.969)
  waiting for transfers between devices: 496 us -> 451 us
  starting transfers between devices: 0.16 us -> 21.3 us
    all_gather x1 -> x0, waiting for transfers between devices: 139 us -> none  [per_device(): all_panels = lax.all_gather(features, 'rows', axis=1, tiled=True)]
    all_to_all x0 -> x1, waiting for transfers between devices: none -> 94.7 us  [per_device(): lax.all_to_all(jnp.stack([features] * lax.axis_size('rows')), 'rows', 0, 0)]
    all_to_all x0 -> x1, starting transfers between devices: none -> 21.1 us  [per_device(): lax.all_to_all(jnp.stack([features] * lax.axis_size('rows')), 'rows', 0, 0)]
  transfers between devices with their start and end apart: 4 -> 4, of which waited for: 4 -> 4; matrix products, arithmetic and copies ran while one was open for 1% -> 0% of each run, Pallas kernels for 0% -> 0%
where the time goes in v1:
time: 778 us; the launch traced here: 777 us
  waiting for transfers between devices  451 us (58%)
  blocking collectives  261 us (34%)
  starting transfers between devices  21.3 us (3%)
  between operations  14.5 us (2%)
  other arithmetic  14 us (2%)
  local copies, waits for them, and re-layouts  9.05 us (1%)
    psum x1, waiting for transfers between devices, per_device(): weight_grad, bias_grad = lax.psum((weight_part, bias_part), 'rows')  326 us
    psum x1, blocking collectives, per_device(): weight_grad, bias_grad = lax.psum((weight_part, bias_part), 'rows')  251 us
    all_to_all x1, waiting for transfers between devices, per_device(): lax.all_to_all(jnp.stack([features] * lax.axis_size('rows')), 'rows', 0, 0)  94.7 us
    reduce_scatter x1, waiting for transfers between devices, per_device(): lax.psum_scatter(partial_grad, 'cols', scatter_dimension=0, tiled=True)  24.1 us
    all_to_all x1, starting transfers between devices, per_device(): lax.all_to_all(jnp.stack([features] * lax.axis_size('rows')), 'rows', 0, 0)  21.1 us
  transfers between devices with their start and end apart: 4, of which 4 were waited for; matrix products, arithmetic and copies ran while one was open for 0% of the time, Pallas kernels for 0%

profile of v1, /device:TPU:1, one launch (start us, length us, event | category | flops | bytes accessed | tf_op | source)
XLA Modules:
  0.0 776.9 jit_solution(3827986943739146926)
XLA Ops:
  7.2 2.7 stack.2
  9.9 21.1 %all-to-all-start = ((bf16[128,64,128]{2,1,0:T(8,128)(2,1)}), bf16[128,64,128]{2,1,0:T(8,128)(2,1)}, u32[]{:S(2)}, u32[]{:S(2)}) async-start(bf16[128,64,128]{2,1,0:T(8,128)(2,1)} %stack.2), calls=%async_computation | async-start | bytes 4194304 | tf_op jit(solution)/shard_map/all_to_all | solution.py:30
  31.0 0.0 reduce-scatter.3.cloned.1.call-start
  31.7 0.1 dynamic_slice.7
  31.9 94.7 %all-to-all-done = bf16[128,64,128]{2,1,0:T(8,128)(2,1)} async-done(((bf16[128,64,128]{2,1,0:T(8,128)(2,1)}), bf16[128,64,128]{2,1,0:T(8,128)(2,1)}, u32[]{:S(2)}, u32[]{:S(2)}) %all-to-all-start) | async-done | bytes 2097184 | tf_op jit(solution)/shard_map/all_to_all | solution.py:30
  126.6 2.3 gather_fusion
  129.0 0.9 fusion.10
  129.9 9.3 %all_gather.3 = bf16[256,128]{1,0:T(8,128)(2,1)S(1)} all-gather(bf16[64,128]{1,0:T(8,128)(2,1)S(1)} %fusion.10), channel_id=1, replica_groups=mesh['rows'=128,'cols'=4] {'cols'}, dimensions={0}, use_global_device_ids=true | all-gather | bytes 81920 | tf_op jit(solution)/shard_map/all_gather | solution.py:35
  139.2 0.9 convert_reduce_fusion
  140.1 0.8 fusion.20
  140.9 0.0 reduce-scatter.3.cloned.1.call-update
  141.0 0.0 reduce-scatter.5.cloned.1.call-start
  141.0 24.1 %reduce-scatter.3.cloned.1.call-done = f32[64,128]{1,0:T(8,128)} async-done(((f32[256,128]{1,0:T(8,128)}), f32[64,128]{1,0:T(8,128)}) %reduce-scatter.3.cloned.1.call-update) | async-done | bytes 32784 | tf_op jit(solution)/shard_map/reduce_scatter | solution.py:54
  165.2 2.5 fusion
  167.7 2.5 broadcast_in_dim.40
  170.2 12.6 %scatter_fusion = f32[128,64,128]{2,1,0:T(8,128)} fusion(f32[128,64,128]{2,1,0:T(8,128)} %broadcast_in_dim.40, s32[65]{0:T(128)S(1)} %fusion.26, f32[65,64,128]{2,1,0:T(8,128)} %fusion), kind=kCustom, calls=%fused_computation.1 | custom fusion | flops 532480 | bytes 6390020 | tf_op jit(solution)/shard_map/scatter-add | solution.py:75
  182.8 0.0 all-reduce.2.cloned.1.call-start
  182.9 251.3 %psum.15 = f32[64]{0:T(128)} all-reduce(f32[64]{0:T(128)S(1)} %broadcast_multiply_fusion), channel_id=1, replica_groups=mesh['rows'=128,'cols'=4] {'rows'}, use_global_device_ids=true, to_apply=%region_5.6 | all-reduce | flops 64 | bytes 512 | tf_op jit(solution)/shard_map/psum | solution.py:63
  434.2 0.8 convolution_multiply_fusion
  435.0 0.0 all-reduce.2.cloned.1.call-update
  435.0 6.5 reduce-scatter.5.cloned.1.call-done
  441.5 1.4 convert_bitcast_fusion
  442.8 326.1 %all-reduce.2.cloned.1.call-done = f32[64,256]{1,0:T(8,128)} async-done(((f32[64,256]{1,0:T(8,128)}), f32[64,256]{1,0:T(8,128)}) %all-reduce.2.cloned.1.call-update) | async-done | bytes 65552 | tf_op jit(solution)/shard_map/psum | solution.py:63
  768.9 1.5 copy.14
  (18 shorter events, 0.1 us)
Async XLA Ops:
  7.2 121.8 %copy-start = (bf16[1,65,128,128]{3,2,1,0:T(8,128)(2,1)S(1)}, bf16[1,65,128,128]{3,2,1,0:T(8,128)(2,1)}, u32[]{:S(2)}) copy-start(bf16[1,65,128,128]{3,2,1,0:T(8,128)(2,1)} %param.10) | copy-start | bytes 6389764
  9.9 21.9 %copy-start.3 = (f32[256]{0:T(256)S(1)}, f32[256]{0:T(256)}, u32[]{:S(2)}) copy-start(f32[256]{0:T(256)} %param.9) | copy-start | bytes 3076
  9.9 21.9 %copy-start.4 = (s32[1,65]{1,0:T(1,128)S(1)}, s32[1,65]{1,0:T(1,128)}, u32[]{:S(2)}) copy-start(s32[1,65]{1,0:T(1,128)} %param.11) | copy-start | bytes 784
  9.9 116.7 %all-to-all-start = ((bf16[128,64,128]{2,1,0:T(8,128)(2,1)}), bf16[128,64,128]{2,1,0:T(8,128)(2,1)}, u32[]{:S(2)}, u32[]{:S(2)}) async-start(bf16[128,64,128]{2,1,0:T(8,128)(2,1)} %stack.2), calls=%async_computation | async-start | bytes 4194304 | tf_op jit(solution)/shard_map/all_to_all | solution.py:30
  31.0 134.2 %reduce-scatter.3.cloned.1.call-start = ((), (), s32[]{:S(2)}) async-start(), calls=%async_computation.3 | async-start | bytes 163840 | tf_op jit(solution)/shard_map/reduce_scatter | solution.py:54
  128.9 10.3 %copy-start.1 = (bf16[256,256]{1,0:T(8,128)(2,1)S(1)}, bf16[256,256]{1,0:T(8,128)(2,1)}, u32[]{:S(2)}) copy-start(bf16[256,256]{1,0:T(8,128)(2,1)} %param.8) | copy-start | bytes 393220
  129.0 10.3 %copy-start.2 = (bf16[64,128]{1,0:T(8,128)(2,1)S(1)}, bf16[64,128]{1,0:T(8,128)(2,1)}, u32[]{:S(2)}) copy-start(bf16[64,128]{1,0:T(8,128)(2,1)} %param.13) | copy-start | bytes 49156
  141.0 300.5 %reduce-scatter.5.cloned.1.call-start = ((), (), s32[]{:S(2)}) async-start(), calls=%async_computation.4 | async-start | bytes 4227072 | tf_op jit(solution)/shard_map/reduce_scatter | solution.py:74
  182.8 586.1 %all-reduce.2.cloned.1.call-start = ((), (), s32[]{:S(2)}) async-start(), calls=%async_computation.5 | async-start | bytes 131072 | tf_op jit(solution)/shard_map/psum | solution.py:63
Sparse Core Ops, SparseCore 0:
  141.1 24.0 reduce-scatter.2
  182.9 258.4 reduce-scatter.4
  445.5 323.3 all-reduce.1
